TPU v7x, 256 devices: a whole 4x4x8 slice. The times are simulated.
256 devices in a mesh: ka: 64 (over z, y, core), pb: 4 (over x).
Axes of the slice: x: 4, y: 4, z: 8, core: 2. Of those that a mesh axis runs over, the one named last changes fastest.
Arguments:
- occupation: float32 [6, 262144], P(None, 'ka'), may hold values from 0 to 1
- gain_table: bfloat16 [64, 36, 262144], P('pb', None, 'ka'), may hold values from 0.0049743652 to 0.19921875
- loss_table: bfloat16 [64, 36, 262144], P('pb', None, 'ka'), may hold values from 0.0049743652 to 0.19921875
- owner: int32 [4, 64, 16, 32, 1], P('pb', 'ka'), may hold values from 0 to 63; in each aligned block of 512 rows (0 to 511, 512 to 1023, ..., all dimensions but the last counted through in order) at most 16 rows name the same one
- local_index: int32 [4, 64, 16, 32], P('pb', 'ka'), may hold values from 0 to 31
- pair_mask: int32 [64, 36], P('pb'), may hold values 0 or 1
- counts: int32 [4, 64], P('pb', 'ka'), may hold values from 1 to 16, as said below
Outputs:
- collision: float32 [6, 262144], P(None, ('ka', 'pb'))
- section_occupation: float32 [6, 262144], P(None, ('ka', 'pb'))
Inputs may be any that keep to these rules, and one draw needn't show every extreme that they name: Among the 16 x 32 entries of one q-shift group and one k-block, no owner is named more than 16 times. The active q-shifts of a group at a k-block are its first counts ones.
All inputs are finite; a program needn't handle non-finite values. No bound on the sum of `pair_mask` on one device may be relied on, other than what follows from the above.
Results may differ from a plain program's by a relative error of at most 0.0003.
Values sent between devices are 32-bit elements; how exact they have to be, the bound alone decides.
No kernel may reach another device: no remote copies, remote signals or barrier semaphores. Data moves between devices by JAX's collectives and lax.ppermute only.
A program may use at most 128 MiB of HBM per device.

v0:
```python
import jax
import jax.numpy as jnp
from jax import lax
from jax.sharding import PartitionSpec as P

half_step = 0.5


def body(occupation, gain_table, loss_table, owner, local_index, pair_mask, counts):
    bands, width = occupation.shape
    shifts = gain_table.shape[0]
    sub_count = local_index.shape[3]
    sub_width = width // sub_count
    ka_count = lax.axis_size("ka")
    total_requests = shifts * sub_count
    owners = owner.reshape(total_requests)
    sources = local_index.reshape(total_requests)
    whole = lax.all_gather(occupation, "ka", axis=1, tiled=True)
    pieces = whole.reshape(bands, ka_count * sub_count, sub_width)
    picked = jnp.take(pieces, owners * sub_count + sources, axis=1).transpose(1, 0, 2)
    shifted = (
        picked.reshape(shifts, sub_count, bands, sub_width)
        .transpose(0, 2, 1, 3)
        .reshape(shifts, bands, width)
    )
    active = (jnp.arange(shifts, dtype=jnp.int32) < counts.reshape(())).astype(jnp.float32)
    weight = pair_mask.astype(jnp.float32) * active[:, None]
    gain_four = (gain_table.astype(jnp.float32) * weight[:, :, None]).reshape(
        shifts, bands, bands, width
    )
    loss_four = (loss_table.astype(jnp.float32) * weight[:, :, None]).reshape(
        shifts, bands, bands, width
    )
    inflow = jnp.einsum("smnk,snk->mk", gain_four, shifted)
    outflow = jnp.einsum("smnk,snk->mk", loss_four, 1.0 - shifted)
    partial_terms = (1.0 - occupation) * inflow - occupation * outflow
    collision = lax.psum_scatter(partial_terms, "pb", scatter_dimension=1, tiled=True)
    share_width = collision.shape[1]
    own_share = lax.dynamic_slice_in_dim(
        occupation, lax.axis_index("pb") * share_width, share_width, 1
    )
    return (collision, own_share + half_step * collision)


def solution(mesh):
    return jax.shard_map(
        body,
        mesh=mesh,
        in_specs=(
            P(None, "ka"),
            P("pb", None, "ka"),
            P("pb", None, "ka"),
            P("pb", "ka", None, None, None),
            P("pb", "ka", None, None),
            P("pb", None),
            P("pb", "ka"),
        ),
        out_specs=(P(None, ("ka", "pb")), P(None, ("ka", "pb"))),
        check_vma=False,
    )
```

profile of v0, /device:TPU:8, one launch (start us, length us, event | category | flops | bytes accessed | tf_op | source)
XLA Modules:
  0.0 143.5 jit_solution(18443966641634054089)
XLA Ops:
  7.2 0.0 all-gather.2.cloned.1.call-start
  7.2 0.7 all-gather.2.cloned.1.call-update
  7.9 0.0 reduce-scatter.2.cloned.1.call-start
  7.9 0.8 reshape.77
  8.7 0.8 reshape.75
  9.5 0.7 fusion.1
  10.2 0.1 mul.61
  10.3 0.1 mul.60
  11.0 0.8 convert_multiply_fusion.2
  11.8 0.1 copy.10
  11.9 13.3 %convert_multiply_fusion.1 = (f32[16,36,4096]{2,0,1:T(8,128)}, f32[16,36,4096]{2,0,1:T(8,128)}) fusion(bf16[16,36,4096]{2,0,1:T(8,128)(2,1)} %param.8, f32[16,36]{0,1:T(8,128)S(1)} %copy.10, bf16[16,36,4096]{2,0,1:T(8,128)(2,1)} %param.9), kind=kLoop, calls=%fused_computation.4 | loop fusion | flops 9437184 | bytes 28313856 | tf_op jit(solution)/shard_map/mul | solution.py:28
  25.2 70.2 %all-gather.2.cloned.1.call-done = f32[6,262144]{1,0:T(8,128)} async-done(((f32[6,4096]{1,0:T(8,128)}), f32[6,262144]{1,0:T(8,128)}) %all-gather.2.cloned.1.call-update) | async-done | bytes 6291472 | tf_op jit(solution)/shard_map/all_gather | solution.py:18
  95.4 4.4 %gather_fusion = f32[512,6,128]{2,1,0:T(8,128)S(1)} fusion(f32[6,2048,128]{2,0,1:T(8,128)} %bitcast.36, s32[1024]{0:T(1024)S(1)} %pad_clamp_fusion), kind=kCustom, calls=%fused_computation | custom fusion | bytes 3147776 | tf_op jit(solution)/shard_map/jit(_take)/gather | solution.py:20
  99.8 1.7 %broadcast_select_fusion = f32[512,6,128]{2,1,0:T(8,128)S(1)} fusion(f32[512,6,128]{2,1,0:T(8,128)S(1)} %gather_fusion, pred[512]{0:T(512)(128)(4,1)S(1)} %compare_and_fusion), kind=kLoop, calls=%fused_computation.6 | loop fusion | flops 393216 | bytes 3146240 | tf_op jit(solution)/shard_map/jit(_take)/select_n | solution.py:20
  101.6 0.2 subtract_bitcast_fusion
  101.8 0.9 copy.24
  102.7 0.9 copy.23
  103.6 0.0 copy-start
  103.7 9.4 %multiply_reduce_fusion = (f32[4096,6]{0,1:T(8,128)S(1)}, f32[4096,6]{0,1:T(8,128)S(1)}) fusion(f32[4096,6,16,6]{0,2,1,3:T(8,128)} %bitcast.33, f32[4096,6,16]{0,2,1:T(8,128)S(1)} %copy.24, f32[4096,6,16,6]{0,2,1,3:T(8,128)} %bitcast.32, f32[4096,6,16]{0,2,1:T(8,128)S(1)} %copy.23), kind=kLoop, calls=%fused_computation.1 | loop fusion | flops 9388032 | bytes 22216704 | tf_op jit(solution)/shard_map/smnk,snk->mk/dot_general | solution.py:35
  113.1 0.0 copy-done
  113.1 0.7 fusion
  113.7 0.0 reduce-scatter.2.cloned.1.call-update
  113.8 21.5 %reduce-scatter.2.cloned.1.call-done = f32[6,1024]{1,0:T(8,128)} async-done(((f32[6,4096]{1,0:T(8,128)}), f32[6,1024]{1,0:T(8,128)}) %reduce-scatter.2.cloned.1.call-update) | async-done | bytes 24592 | tf_op jit(solution)/shard_map/reduce_scatter | solution.py:37
  135.3 1.4 multiply_add_fusion
  (4 shorter events, 0.0 us)
Async XLA Ops:
  7.2 88.3 %all-gather.2.cloned.1.call-start = ((), (), s32[]{:S(2)}) async-start(), calls=%async_computation.1 | async-start | bytes 8519680 | tf_op jit(solution)/shard_map/all_gather | solution.py:18
  7.9 127.4 %reduce-scatter.2.cloned.1.call-start = ((), (), s32[]{:S(2)}) async-start(), calls=%async_computation.2 | async-start | bytes 163840 | tf_op jit(solution)/shard_map/reduce_scatter | solution.py:37
  103.6 9.4 %copy-start = (f32[6,4096]{1,0:T(8,128)S(1)}, f32[6,4096]{1,0:T(8,128)}, u32[]{:S(2)}) copy-start(f32[6,4096]{1,0:T(8,128)} %param.7) | copy-start | bytes 294916
Sparse Core Ops, SparseCore 0:
  10.8 84.6 all-gather.1
  113.9 21.3 reduce-scatter.1
where the time goes:
time: 144 us; the launch traced here: 143 us
  waiting for transfers between devices  92.4 us (64%)
  other arithmetic  28.2 us (20%)
  between operations  14.8 us (10%)
  local copies, waits for them, and re-layouts  7.99 us (6%)
    all_gather x1, waiting for transfers between devices, body(): whole = lax.all_gather(occupation, 'ka', axis=1, tiled=True)  70.2 us
    reduce_scatter x1, waiting for transfers between devices, body(): lax.psum_scatter(partial_terms, 'pb', scatter_dimension=1, tiled=True)  21.5 us
    mul x1, other arithmetic, body(): gain_table.astype(jnp.float32) * weight[:, :, None]  13.3 us
    dot_general x1, other arithmetic, body(): outflow = jnp.einsum('smnk,snk->mk', loss_four, 1.0 - shifted)  9.4 us
    gather x1, local copies, waits for them, and re-layouts, body(): jnp.take(pieces, owners * sub_count + sources, axis=1).transpose(1, 0, 2)  4.36 us
  transfers between devices with their start and end apart: 2, of which 2 were waited for; matrix products, arithmetic and copies ran while one was open for 12% of the time, Pallas kernels for 0%

commit v1 on v0

--- a/solution.py
+++ b/solution.py
@@ -15,7 +15,9 @@
     total_requests = shifts * sub_count
     owners = owner.reshape(total_requests)
     sources = local_index.reshape(total_requests)
-    whole = lax.all_gather(occupation, "ka", axis=1, tiled=True)
+    whole = jnp.concatenate(
+        lax.all_to_all(jnp.stack([occupation] * lax.axis_size("ka")), "ka", 0, 0), axis=1
+    )
     pieces = whole.reshape(bands, ka_count * sub_count, sub_width)
     picked = jnp.take(pieces, owners * sub_count + sources, axis=1).transpose(1, 0, 2)
     shifted = (

time: 144 us -> 258 us (1.79)
  waiting for transfers between devices: 92.4 us -> 192 us
  starting transfers between devices: 0.08 us -> 12.5 us
  local copies, waits for them, and re-layouts: 7.99 us -> 11.8 us
    all_to_all x0 -> x1, waiting for transfers between devices: none -> 170 us  [body(): lax.all_to_all(jnp.stack([occupation] * lax.axis_size('ka')), 'ka', 0, 0)]
    all_gather x1 -> x0, waiting for transfers between devices: 70.2 us -> none  [body(): whole = lax.all_gather(occupation, 'ka', axis=1, tiled=True)]
    all_to_all x0 -> x1, starting transfers between devices: none -> 12.4 us  [body(): lax.all_to_all(jnp.stack([occupation] * lax.axis_size('ka')), 'ka', 0, 0)]
    another operation x0 -> x1, local copies, waits for them, and re-layouts: none -> 5.19 us  [body(): jnp.stack([occupation] * lax.axis_size('ka'))]
  transfers between devices with their start and end apart: 2 -> 2, of which waited for: 2 -> 2; matrix products, arithmetic and copies ran while one was open for 12% -> 5% of each run, Pallas kernels for 0% -> 0%
where the time goes in v1:
time: 258 us
  waiting for transfers between devices  192 us (74%)
  other arithmetic  26.8 us (10%)
  between operations  14.8 us (6%)
  starting transfers between devices  12.5 us (5%)
  local copies, waits for them, and re-layouts  11.8 us (5%)
    all_to_all x1, waiting for transfers between devices, body(): lax.all_to_all(jnp.stack([occupation] * lax.axis_size('ka')), 'ka', 0, 0)  170 us
    reduce_scatter x1, waiting for transfers between devices, body(): lax.psum_scatter(partial_terms, 'pb', scatter_dimension=1, tiled=True)  21.3 us
    mul x1, other arithmetic, body(): gain_table.astype(jnp.float32) * weight[:, :, None]  13.3 us
    all_to_all x1, starting transfers between devices, body(): lax.all_to_all(jnp.stack([occupation] * lax.axis_size('ka')), 'ka', 0, 0)  12.4 us
    dot_general x1, other arithmetic, body(): outflow = jnp.einsum('smnk,snk->mk', loss_four, 1.0 - shifted)  9.4 us
    another operation x1, local copies, waits for them, and re-layouts, body(): jnp.stack([occupation] * lax.axis_size('ka'))  5.19 us
  transfers between devices with their start and end apart: 2, of which 2 were waited for; matrix products, arithmetic and copies ran while one was open for 5% of the time, Pallas kernels for 0%

profile of v1, /device:TPU:8, one launch (start us, length us, event | category | flops | bytes accessed | tf_op | source)
XLA Modules:
  0.0 257.6 jit_solution(12326985874030446899)
XLA Ops:
  7.2 5.2 %stack.2 = f32[64,6,4096]{2,1,0:T(8,128)} broadcast(f32[6,4096]{1,0:T(8,128)} %param.7), dimensions={1,2} | broadcast | bytes 6389760 | tf_op jit(solution)/shard_map/stack | solution.py:19
  12.4 0.0 copy-start.1
  12.4 0.0 copy-start.2
  12.4 0.0 copy-start.3
  12.4 12.4 %all-to-all-start = ((f32[64,6,4096]{2,1,0:T(8,128)}), f32[64,6,4096]{2,1,0:T(8,128)}, u32[]{:S(2)}, u32[]{:S(2)}) async-start(f32[64,6,4096]{2,1,0:T(8,128)} %stack.2), calls=%async_computation | async-start | bytes 16777216 | tf_op jit(solution)/shard_map/all_to_all | solution.py:19
  24.8 0.0 reduce-scatter.2.cloned.1.call-start
  24.8 0.0 copy-done.1
  24.8 0.1 reshape.79
  24.9 0.1 reshape.77
  25.0 0.0 copy-done.2
  25.0 0.1 mul.61
  25.1 0.1 mul.60
  25.9 0.0 copy-done.3
  25.9 0.1 convert_multiply_fusion.2
  25.9 0.1 copy.14
  26.1 13.3 %convert_multiply_fusion.1 = (f32[16,36,4096]{2,0,1:T(8,128)}, f32[16,36,4096]{2,0,1:T(8,128)}) fusion(bf16[16,36,4096]{2,0,1:T(8,128)(2,1)} %param.8, f32[16,36]{0,1:T(8,128)S(1)} %copy.14, bf16[16,36,4096]{2,0,1:T(8,128)(2,1)} %param.9), kind=kLoop, calls=%fused_computation.4 | loop fusion | flops 9437184 | bytes 28313856 | tf_op jit(solution)/shard_map/mul | solution.py:30
  39.3 170.5 %all-to-all-done = f32[64,6,4096]{2,1,0:T(8,128)} async-done(((f32[64,6,4096]{2,1,0:T(8,128)}), f32[64,6,4096]{2,1,0:T(8,128)}, u32[]{:S(2)}, u32[]{:S(2)}) %all-to-all-start) | async-done | bytes 6291488 | tf_op jit(solution)/shard_map/all_to_all | solution.py:19
  209.8 4.4 %gather_fusion = f32[512,6,128]{2,1,0:T(8,128)S(1)} fusion(f32[6,2048,128]{2,0,1:T(8,128)} %bitcast.5, s32[1024]{0:T(1024)S(1)} %pad_clamp_fusion), kind=kCustom, calls=%fused_computation | custom fusion | bytes 3147776 | tf_op jit(solution)/shard_map/jit(_take)/gather | solution.py:22
  214.2 1.7 broadcast_select_fusion
  215.9 0.2 subtract_bitcast_fusion
  216.2 0.9 copy.28
  217.1 0.9 copy.27
  218.0 0.0 copy-start
  218.0 9.4 %multiply_reduce_fusion = (f32[4096,6]{0,1:T(8,128)S(1)}, f32[4096,6]{0,1:T(8,128)S(1)}) fusion(f32[4096,6,16,6]{0,2,1,3:T(8,128)} %bitcast.35, f32[4096,6,16]{0,2,1:T(8,128)S(1)} %copy.28, f32[4096,6,16,6]{0,2,1,3:T(8,128)} %bitcast.34, f32[4096,6,16]{0,2,1:T(8,128)S(1)} %copy.27), kind=kLoop, calls=%fused_computation.1 | loop fusion | flops 9388032 | bytes 22216704 | tf_op jit(solution)/shard_map/smnk,snk->mk/dot_general | solution.py:37
  227.4 0.0 copy-done
  227.4 0.7 fusion
  228.1 0.0 reduce-scatter.2.cloned.1.call-update
  228.1 21.3 %reduce-scatter.2.cloned.1.call-done = f32[6,1024]{1,0:T(8,128)} async-done(((f32[6,4096]{1,0:T(8,128)}), f32[6,1024]{1,0:T(8,128)}) %reduce-scatter.2.cloned.1.call-update) | async-done | bytes 24592 | tf_op jit(solution)/shard_map/reduce_scatter | solution.py:39
  249.4 1.4 multiply_add_fusion
  (5 shorter events, 0.1 us)
Async XLA Ops:
  12.4 12.5 %copy-start.1 = (s32[1,1,16,32]{3,2,1,0:T(8,128)S(1)}, s32[1,1,16,32]{3,2,1,0:T(8,128)}, u32[]{:S(2)}) copy-start(s32[1,1,16,32]{3,2,1,0:T(8,128)} %param.11) | copy-start | bytes 6148
  12.4 12.7 %copy-start.2 = (s32[1,1,16,32,1]{3,4,2,1,0:T(1,128)S(1)}, s32[1,1,16,32,1]{3,4,2,1,0:T(1,128)}, u32[]{:S(2)}) copy-start(s32[1,1,16,32,1]{3,4,2,1,0:T(1,128)} %param.10) | copy-start | bytes 6148
  12.4 13.5 %copy-start.3 = (s32[16,36]{1,0:T(8,128)S(1)}, s32[16,36]{1,0:T(8,128)}, u32[]{:S(2)}) copy-start(s32[16,36]{1,0:T(8,128)} %param.12) | copy-start | bytes 6916
  12.4 197.4 %all-to-all-start = ((f32[64,6,4096]{2,1,0:T(8,128)}), f32[64,6,4096]{2,1,0:T(8,128)}, u32[]{:S(2)}, u32[]{:S(2)}) async-start(f32[64,6,4096]{2,1,0:T(8,128)} %stack.2), calls=%async_computation | async-start | bytes 16777216 | tf_op jit(solution)/shard_map/all_to_all | solution.py:19
  24.8 224.6 %reduce-scatter.2.cloned.1.call-start = ((), (), s32[]{:S(2)}) async-start(), calls=%async_computation.2 | async-start | bytes 163840 | tf_op jit(solution)/shard_map/reduce_scatter | solution.py:39
  218.0 9.4 %copy-start = (f32[6,4096]{1,0:T(8,128)S(1)}, f32[6,4096]{1,0:T(8,128)}, u32[]{:S(2)}) copy-start(f32[6,4096]{1,0:T(8,128)} %param.7) | copy-start | bytes 294916
Sparse Core Ops, SparseCore 0:
  228.2 21.1 reduce-scatter.1
